TPU v7x, 32 devices: a whole 2x2x4 slice. The times are simulated.
32 devices in a mesh: section: 4 (over y, x), tp: 4 (over z), mirror: 2 (over core).
Axes of the slice: x: 2, y: 2, z: 4, core: 2. Of those that a mesh axis runs over, the one named last changes fastest.
Arguments:
- feats: bfloat16 [2, 2, 128, 5120], P('mirror', None, 'tp'), may hold values from -16 to 16
- types: int32 [2, 2, 128], P('mirror', None, 'tp'), may hold values from 0 to 63
- segs: int32 [2, 2, 5, 128], P('mirror'), may hold values from 0 to 3, never falling along the last dimension, each value on 1 to 64 neighbouring positions
- type_table: bfloat16 [64, 5120], replicated, may hold values from -3 to 3
- gains: float32 [2, 4, 5120], P('mirror', 'section'), may hold values from 0.25 to 1.75, as said below
- w_qkv: bfloat16 [2, 4, 3, 5120, 512], P('mirror', 'section', None, None, 'tp'), may hold values from -8 to 8, as said below
- w_out: bfloat16 [2, 4, 512, 5120], P('mirror', 'section', 'tp'), as said below
- carry_acts: bfloat16 [2, 4, 128, 5120], P('mirror', 'section', 'tp'), may hold values from -16 to 16
- grad_in: bfloat16 [2, 4, 128, 5120], P('mirror', 'section', 'tp'), may hold values from -6 to 6
- saved: bfloat16 [2, 4, 2, 128, 5120], P('mirror', 'section', None, 'tp'), may hold values from -16 to 16
- cotangent: bfloat16 [2, 2, 128, 5120], P('mirror', None, 'tp'), may hold values from -6 to 6
Outputs:
- acts: bfloat16 [2, 4, 2, 128, 5120], P('mirror', 'section', None, 'tp')
- grad_acts: bfloat16 [2, 4, 2, 128, 5120], P('mirror', 'section', None, 'tp')
- grad_qkv: bfloat16 [2, 4, 3, 5120, 512], P('mirror', 'section', None, None, 'tp')
- grad_out: bfloat16 [2, 4, 512, 5120], P('mirror', 'section', 'tp')
Inputs may be any that keep to these rules, and one draw needn't show every extreme that they name: w_qkv[1, k] equals w_qkv[0, 3 - k]. w_out[1, k] equals w_out[0, 3 - k]. gains[1, k] equals gains[0, 3 - k]. `segs`: segment numbers never fall along a micro-batch; each segment holds at most half of 128 tokens, and one holds exactly that many.
All inputs are finite; a program needn't handle non-finite values.
Results may differ from a plain program's by a relative error of at most 0.015.
Values may be sent and summed in bfloat16 or wider, within the bound.
No kernel may reach another device: no remote copies, remote signals or barrier semaphores. Data moves between devices by JAX's collectives and lax.ppermute only.
A program may use at most 128 MiB of HBM per device.

v0:
```python
import math
import numpy as np
import jax
import jax.numpy as jnp
from jax import lax
from jax.sharding import PartitionSpec as P

HD = 128


def passed_along(block, axis, distance):
    devices = range(lax.axis_size(axis))
    route = [(i - distance, i) for i in devices if i - distance in devices]
    return lax.ppermute(block, axis, route)


def flipped(value, axis, mask):
    return lax.ppermute(value, axis, [(i, i ^ mask) for i in range(lax.axis_size(axis))])


def normalize(values, gain_row):
    mean_square = jnp.mean(values * values, axis=-1, keepdims=True)
    return values * lax.rsqrt(mean_square + 1e-05) * gain_row


def segment_mask(segment_ids):
    position = jnp.arange(segment_ids.shape[0], dtype=jnp.int32)
    causal = position[None, :] <= position[:, None]
    return causal & (segment_ids[:, None] == segment_ids[None, :])


def attend(queries, keys_all, values_all, seg_mask):
    scores = jnp.einsum(
        "ihd,jhd->hij", queries, keys_all, preferred_element_type=jnp.float32
    ) / math.sqrt(queries.shape[-1])
    scores = jnp.where(seg_mask[None], scores, -1e30)
    highest = lax.stop_gradient(jnp.max(scores, axis=-1, keepdims=True))
    expo = jnp.exp(scores - highest)
    probs = (expo / jnp.sum(expo, axis=-1, keepdims=True)).astype(values_all.dtype)
    return jnp.einsum("hij,jhd->ihd", probs, values_all, preferred_element_type=jnp.float32)


def embedding(feat_rows, type_rows, type_table):
    onehot = (
        type_rows[:, None] == jnp.arange(type_table.shape[0], dtype=jnp.int32)[None, :]
    ).astype(jnp.bfloat16)
    looked = jnp.dot(onehot, type_table, preferred_element_type=jnp.float32)
    return (feat_rows.astype(jnp.float32) + looked).astype(jnp.bfloat16)


def gathered(blocks):
    full = lax.all_gather(jnp.stack(blocks), "tp", axis=1, tiled=True)
    return [full[i] for i in range(len(blocks))]


def scattered(blocks):
    part = lax.psum_scatter(jnp.stack(blocks), "tp", scatter_dimension=1, tiled=True)
    return [part[i] for i in range(len(blocks))]


def shards(
    feats, types, segs, type_table, gains, w_qkv, w_out, carry_acts, grad_in, saved, cotangent
):
    sections = lax.axis_size("section")
    section_index = lax.axis_index("section")
    on_first_pipe = lax.axis_index("mirror") == 0
    position = jnp.where(on_first_pipe, section_index, sections - 1 - section_index)
    gain_row = gains[0, 0]
    qkv_weight = w_qkv[0, 0]
    out_weight = w_out[0, 0]
    window_steps = feats.shape[1]
    seq_len = segs.shape[3]
    model_width = qkv_weight.shape[1]
    inner_here = qkv_weight.shape[-1]
    heads_here = inner_here // HD

    def mask_for(which, index):
        return segment_mask(lax.dynamic_index_in_dim(segs[0, which], index, 0, keepdims=False))

    def normed_rows(rows):
        return normalize(rows.astype(jnp.float32), gain_row).astype(jnp.bfloat16)

    def heads_of(normed_full):
        projected = jnp.einsum(
            "sd,cdn->csn", normed_full, qkv_weight, preferred_element_type=jnp.float32
        ).astype(jnp.bfloat16)
        return projected.reshape(3, seq_len, heads_here, HD)

    def forward_part(normed_full, seg_mask, heads_view=None):
        if heads_view is None:
            heads_view = heads_of(normed_full)
        mixed = (
            attend(heads_view[0], heads_view[1], heads_view[2], seg_mask)
            .reshape(seq_len, inner_here)
            .astype(jnp.bfloat16)
        )
        return mixed

    def backward_part(normed_full, upstream_full, seg_mask, heads_view=None):
        if heads_view is None:
            heads_view = heads_of(normed_full)
        primal, pull_attend = jax.vjp(
            lambda query_part, key_part, value_part: attend(
                query_part, key_part, value_part, seg_mask
            ),
            heads_view[0],
            heads_view[1],
            heads_view[2],
        )
        mixed = primal.reshape(seq_len, inner_here).astype(jnp.bfloat16)
        d_mixed = jnp.einsum(
            "sd,nd->sn", upstream_full, out_weight, preferred_element_type=jnp.float32
        ).astype(jnp.bfloat16)
        pulled = pull_attend(d_mixed.astype(jnp.float32).reshape(seq_len, heads_here, HD))
        d_projected = jnp.stack(pulled).reshape(3, seq_len, inner_here)
        return (d_projected, mixed)

    qkv_rows = jnp.transpose(qkv_weight, (0, 2, 1)).reshape(3 * inner_here, model_width)
    padded_out = jnp.concatenate(
        [out_weight, jnp.zeros((2 * inner_here, model_width), out_weight.dtype)], axis=0
    )
    block_weight = jnp.stack([qkv_rows, padded_out])

    def projected_back(d_projected, forward_mixed):
        lhs = jnp.stack(
            [
                jnp.transpose(d_projected, (1, 0, 2)).reshape(seq_len, 3 * inner_here),
                jnp.concatenate(
                    [forward_mixed, jnp.zeros((seq_len, 2 * inner_here), forward_mixed.dtype)],
                    axis=1,
                ),
            ]
        )
        return jnp.einsum(
            "tsk,tkd->tsd", lhs, block_weight, preferred_element_type=jnp.float32
        ).astype(jnp.bfloat16)

    def weight_terms(normed_fulls, d_projecteds, mixeds, upstream_fulls):
        qkv_sum = None
        out_sum = None
        for normed_full, d_projected, mixed, upstream_full in zip(
            normed_fulls, d_projecteds, mixeds, upstream_fulls
        ):
            qkv_term = jnp.einsum(
                "sd,csn->cdn", normed_full, d_projected, preferred_element_type=jnp.float32
            )
            out_term = jnp.einsum(
                "sn,sd->nd", mixed, upstream_full, preferred_element_type=jnp.float32
            )
            qkv_sum = qkv_term if qkv_sum is None else qkv_sum + qkv_term
            out_sum = out_term if out_sum is None else out_sum + out_term
        return (qkv_sum.astype(jnp.bfloat16), out_sum.astype(jnp.bfloat16))

    def input_grad(layer_in, upstream, d_normed):
        unused_norm, pull_norm = jax.vjp(
            lambda inputs: normalize(inputs, gain_row), layer_in.astype(jnp.float32)
        )
        d_input = pull_norm(d_normed.astype(jnp.float32))[0]
        return (upstream.astype(jnp.float32) + d_input).astype(jnp.bfloat16)

    pair_axes = ("section", "mirror")
    mirror_size = lax.axis_size("mirror")
    up_pairs = []
    down_pairs = []
    for section in range(sections):
        for mirror in range(mirror_size):
            ahead = 1 if mirror == 0 else -1
            if 0 <= section + ahead < sections:
                up_pairs.append(
                    (section * mirror_size + mirror, (section + ahead) * mirror_size + mirror)
                )
            if 0 <= section - ahead < sections:
                down_pairs.append(
                    (section * mirror_size + mirror, (section - ahead) * mirror_size + mirror)
                )
    bit_count = lax.axis_size(pair_axes).bit_length() - 1
    section_bits = list(range(1, bit_count))
    if section_bits:
        routes = []
        for start in range(len(section_bits)):
            order = section_bits[start:] + section_bits[:start]
            routes.append([1 | 1 << order[0]] + [1 << bit for bit in order[1:]])
    else:
        routes = [[1]]

    def to_partner(value):
        return flipped(value, pair_axes, (1 << bit_count) - 1)

    last_step = window_steps - 1
    saved_normed = [normed_rows(saved[0, 0, t]) for t in range(window_steps)]
    backward_normed_full = [None] * window_steps
    upstream_fulls = []
    d_projecteds = []
    mixeds = []
    partner_normed = [None] * window_steps
    partner_upstream = []
    partner_d_projected = []
    partner_mixed = []
    forward_outs = []
    backward_outs = []
    forward_in = carry_acts[0, 0]
    backward_in = grad_in[0, 0]
    inbox = {}
    deferred = {}
    tie_scatter = {}
    for step_index in range(window_steps):
        embedded = embedding(feats[0, step_index], types[0, step_index], type_table)
        current = jnp.where(position == 0, embedded, forward_in)
        upstream = jnp.where(position == sections - 1, cotangent[0, step_index], backward_in)
        if step_index == 0:
            upstream_full, backward_normed_full[0], forward_normed_full = gathered(
                [upstream, saved_normed[0], normed_rows(current)]
            )
            first_sent = to_partner(jnp.stack([upstream_full, backward_normed_full[0]]))
            paired = jnp.einsum(
                "tsd,cdn->tcsn",
                jnp.stack([backward_normed_full[0], forward_normed_full]),
                qkv_weight,
                preferred_element_type=jnp.float32,
            ).astype(jnp.bfloat16)
            step_heads = [paired[t].reshape(3, seq_len, heads_here, HD) for t in range(2)]
        else:
            step_heads = [None, None]
            upstream_full, forward_normed_full = gathered([upstream, normed_rows(current)])
            inbox[f"rows{step_index}"] = to_partner(upstream_full)
        d_projected, mixed = backward_part(
            backward_normed_full[step_index],
            upstream_full,
            mask_for(1, step_index + position),
            step_heads[0],
        )
        upstream_fulls.append(upstream_full)
        d_projecteds.append(d_projected)
        mixeds.append(mixed)
        small = jnp.concatenate([d_projected, mixed[None]])
        if step_index < last_step:
            deferred[f"small{step_index}"] = small
        else:
            inbox[f"small{step_index}"] = to_partner(small)
        forward_mixed = forward_part(
            forward_normed_full, mask_for(0, step_index - position + sections - 1), step_heads[1]
        )
        both_parts, tie_scatter = lax.optimization_barrier(
            (projected_back(d_projected, forward_mixed), tie_scatter)
        )
        inbox.update(tie_scatter)
        tie_scatter = {}
        both_rows = lax.psum_scatter(both_parts, "tp", scatter_dimension=1, tiled=True)
        d_normed, attn_rows = (both_rows[0], both_rows[1])
        if step_index == 0 and window_steps > 1:
            later_rows, d_normed = lax.optimization_barrier((saved_normed[1:], d_normed))
            later = gathered(later_rows)
            backward_normed_full[1:] = later
            deferred["later"] = jnp.stack(later)
        backward_out = input_grad(saved[0, 0, step_index], upstream, d_normed)
        forward_out = (current.astype(jnp.float32) + attn_rows.astype(jnp.float32)).astype(
            jnp.bfloat16
        )
        forward_outs.append(forward_out)
        backward_outs.append(backward_out)
        if step_index < last_step:
            backward_in = lax.ppermute(backward_out, pair_axes, down_pairs)
            forward_in = lax.ppermute(forward_out, pair_axes, up_pairs)
            if step_index == 0:
                deferred, first_sent, backward_in, forward_in = lax.optimization_barrier(
                    (deferred, first_sent, backward_in, forward_in)
                )
                inbox["first"] = first_sent
            else:
                deferred, backward_in, forward_in = lax.optimization_barrier(
                    (deferred, backward_in, forward_in)
                )
            tie_scatter = {key: to_partner(value) for key, value in deferred.items()}
            deferred = {}
    partner_upstream = [inbox["first"][0]] + [inbox[f"rows{t}"] for t in range(1, window_steps)]
    partner_normed = [inbox["first"][1]] + (
        [inbox["later"][t] for t in range(window_steps - 1)] if window_steps > 1 else []
    )
    partner_d_projected = [inbox[f"small{t}"][:3] for t in range(window_steps)]
    partner_mixed = [inbox[f"small{t}"][3] for t in range(window_steps)]
    own_qkv, own_out = weight_terms(backward_normed_full, d_projecteds, mixeds, upstream_fulls)
    other_qkv, other_out = weight_terms(
        partner_normed, partner_d_projected, partner_mixed, partner_upstream
    )
    grad_qkv = (own_qkv.astype(jnp.float32) + other_qkv.astype(jnp.float32)).astype(jnp.bfloat16)
    grad_out = (own_out.astype(jnp.float32) + other_out.astype(jnp.float32)).astype(jnp.bfloat16)
    acts_block = jnp.stack(forward_outs)[None, None]
    grads_block = jnp.stack(backward_outs)[None, None]
    return (acts_block, grads_block, grad_qkv[None, None], grad_out[None, None])


def solution(mesh):
    in_specs = (
        P("mirror", None, "tp", None),
        P("mirror", None, "tp"),
        P("mirror", None, None, None),
        P(),
        P("mirror", "section", None),
        P("mirror", "section", None, None, "tp"),
        P("mirror", "section", "tp", None),
        P("mirror", "section", "tp", None),
        P("mirror", "section", "tp", None),
        P("mirror", "section", None, "tp", None),
        P("mirror", None, "tp", None),
    )
    out_specs = (
        P("mirror", "section", None, "tp", None),
        P("mirror", "section", None, "tp", None),
        P("mirror", "section", None, None, "tp"),
        P("mirror", "section", "tp", None),
    )
    return jax.shard_map(shards, mesh=mesh, in_specs=in_specs, out_specs=out_specs, check_vma=False)
```

profile of v0, /device:TPU:0, one launch (start us, length us, event | category | flops | bytes accessed | tf_op | source)
XLA Modules:
  0.0 318.5 jit_solution(18364899609434030031)
XLA Ops:
  7.3 1.4 slice_bitcast_fusion.59
  8.7 1.5 multiply_reduce_fusion
  10.2 1.3 fusion.72
  11.7 0.9 fusion.91
  12.6 1.1 pad_maximum_fusion.3
  13.8 6.3 %copy.15 = bf16[3,128,5120]{2,1,0:T(8,128)(2,1)} copy(bf16[3,128,5120]{1,2,0:T(8,128)(2,1)} %bitcast.361) | data formatting | bytes 7864320 | tf_op jit(solution)/shard_map/transpose | solution.py:118
  20.6 3.7 %pad_bitcast_fusion = bf16[1,384,5120]{2,1,0:T(8,128)(2,1)} fusion(bf16[128,5120]{1,0:T(8,128)(2,1)} %bitcast.363), kind=kLoop, calls=%fused_computation.28 | loop fusion | bytes 5242880 | tf_op jit(solution)/shard_map/stack | solution.py:122
  24.3 68.7 %all-gather.5.cloned.1.call-done = bf16[3,128,5120]{2,1,0:T(8,128)(2,1)} async-done(((bf16[3,32,5120]{2,1,0:T(8,128)(2,1)}), bf16[3,128,5120]{2,1,0:T(8,128)(2,1)}) %all-gather.5.cloned.1.call-update) | async-done | bytes 3932176 | tf_op jit(solution)/shard_map/all_gather | solution.py:52
  93.0 4.6 %fusion.33 = bf16[2,3,128,128]{3,2,1,0:T(8,128)(2,1)S(1)} fusion(bf16[1,1,3,5120,128]{4,3,2,1,0:T(8,128)(2,1)} %param.16, bf16[3,128,5120]{2,1,0:T(8,128)(2,1)} %all-gather.5.cloned.1.call-done), kind=kOutput, calls=%fused_computation.47 | convolution fusion | flops 1006731264 | bytes 6750208 | tf_op jit(solution)/shard_map/tsd,cdn->tcsn/dot_general | solution.py:215
  97.9 2.0 fusion.68
  101.3 3.0 convolution_convert_fusion.1
  104.3 1.3 fusion.9
  105.6 3.5 %stack.115 = bf16[2,128,5120]{2,1,0:T(8,128)(2,1)} slice(bf16[3,128,5120]{2,1,0:T(8,128)(2,1)} %all-gather.5.cloned.1.call-done), slice={[0:2], [0:128], [0:5120]} | slice | bytes 5242880 | tf_op jit(solution)/shard_map/stack | solution.py:214
  109.1 1.7 collective-permute-start
  110.8 44.5 %reduce-scatter.3.cloned.1.call-done = bf16[2,32,5120]{2,1,0:T(8,128)(2,1)} async-done(((bf16[2,128,5120]{2,1,0:T(8,128)(2,1)}), bf16[2,32,5120]{2,1,0:T(8,128)(2,1)}) %reduce-scatter.3.cloned.1.call-update) | async-done | bytes 655376 | tf_op jit(solution)/shard_map/reduce_scatter | solution.py:248
  155.2 1.0 slice_bitcast_fusion.24
  156.9 1.3 collective-permute-start.1
  158.2 1.0 fusion.90
  159.2 5.3 %collective-permute-start.2 = (bf16[32,5120]{1,0:T(8,128)(2,1)S(1)}, bf16[32,5120]{1,0:T(8,128)(2,1)}, u32[]{:S(2)}, u32[]{:S(2)}) collective-permute-start(bf16[32,5120]{1,0:T(8,128)(2,1)S(1)} %fusion.90), channel_id=1, source_target_pairs={{0,8},{8,16},{9,1},{16,24},{17,9},{25,17},{2,10},{10,18},{11,3},{1... | collective-permute-start | bytes 983048 | tf_op jit(solution)/shard_map/ppermute | solution.py:263
  164.5 0.9 convolution_convert_fusion.8
  166.1 3.3 %collective-permute-done = bf16[2,128,5120]{2,1,0:T(8,128)(2,1)} collective-permute-done((bf16[2,128,5120]{2,1,0:T(8,128)(2,1)}, bf16[2,128,5120]{2,1,0:T(8,128)(2,1)}, u32[]{:S(2)}, u32[]{:S(2)}) %collective-permute-start) | collective-permute-done | bytes 2621472 | tf_op jit(solution)/shard_map/ppermute | solution.py:18
  169.4 6.7 %collective-permute-done.1 = bf16[32,5120]{1,0:T(8,128)(2,1)S(1)} collective-permute-done((bf16[32,5120]{1,0:T(8,128)(2,1)S(1)}, bf16[32,5120]{1,0:T(8,128)(2,1)S(1)}, u32[]{:S(2)}, u32[]{:S(2)}) %collective-permute-start.1) | collective-permute-done | bytes 327712 | tf_op jit(solution)/shard_map/ppermute | solution.py:262
  176.1 13.3 %all-gather.9.cloned.1.call-done = bf16[128,5120]{1,0:T(8,128)(2,1)} async-done(((bf16[32,5120]{1,0:T(8,128)(2,1)}), bf16[128,5120]{1,0:T(8,128)(2,1)}) %all-gather.9.cloned.1.call-update) | async-done | bytes 1310736 | tf_op jit(solution)/shard_map/all_gather | solution.py:52
  189.9 0.9 pad_maximum_fusion.4
  191.1 1.2 collective-permute-start.3
  192.3 1.5 collective-permute-start.4
  193.8 3.0 fusion.44
  197.0 48.9 %all-gather.7.cloned.1.call-done = bf16[2,128,5120]{2,1,0:T(8,128)(2,1)} async-done(((bf16[2,32,5120]{2,1,0:T(8,128)(2,1)}), bf16[2,128,5120]{2,1,0:T(8,128)(2,1)}) %all-gather.7.cloned.1.call-update) | async-done | bytes 2621456 | tf_op jit(solution)/shard_map/all_gather | solution.py:52
  246.0 2.0 fusion.67
  248.1 3.5 %fusion.49 = bf16[3,128,128]{2,1,0:T(8,128)(2,1)S(1)} fusion(bf16[1,1,3,5120,128]{4,3,2,1,0:T(8,128)(2,1)} %param.16, bf16[2,128,5120]{2,1,0:T(8,128)(2,1)} %all-gather.7.cloned.1.call-done), kind=kOutput, calls=%fused_computation.55 | convolution fusion | flops 503365632 | bytes 5341184 | tf_op jit(solution)/shard_map/sd,cdn->csn/dot_general | solution.py:84
  252.9 3.0 convolution_convert_fusion
  256.7 1.8 fusion.31
  258.5 2.6 fusion.18
  261.3 1.7 collective-permute-start.5
  263.0 1.1 slice_bitcast_fusion.6
  264.2 1.0 collective-permute-start.6
  265.8 1.2 add_convert_fusion.2
  266.9 3.4 %fusion.19 = f32[128,5120]{1,0:T(8,128)} fusion(bf16[2,128,5120]{2,1,0:T(8,128)(2,1)} %collective-permute-done, bf16[4,128,128]{1,2,0:T(8,128)(2,1)S(1)} %collective-permute-done.4), kind=kOutput, calls=%fused_computation.35 | convolution fusion | flops 167772160 | bytes 3964928 | tf_op jit(solution)/shard_map/sn,sd->nd/dot_general | solution.py:147
  270.3 2.5 fusion.21
  272.8 4.4 %fusion = bf16[1,1,3,5120,128]{3,4,2,1,0:T(8,128)(2,1)} fusion(f32[3,128,5120]{2,1,0:T(8,128)S(1)} %fusion.21, bf16[4,128,128]{1,2,0:T(8,128)(2,1)S(1)} %collective-permute-done.4, bf16[3,128,5120]{2,1,0:T(8,128)(2,1)S(1)} %add_convert_fusion.2, bf16[2,128,5120]{2,1,0:T(8,128)(2,1)} %collective-permute-done), kind=kOutput, calls=%fused_computation.6 | convolution fusion | flops 515112960 | bytes 17170432 | tf_op jit(solution)/shard_map/sd,csn->cdn/dot_general | solution.py:144
  277.3 6.3 %copy.18 = bf16[1,1,3,5120,128]{4,3,2,1,0:T(8,128)(2,1)} copy(bf16[1,1,3,5120,128]{3,4,2,1,0:T(8,128)(2,1)} %fusion) | data formatting | bytes 7864320
  283.5 11.9 %collective-permute-done.6 = bf16[128,5120]{1,0:T(8,128)(2,1)} collective-permute-done((bf16[128,5120]{1,0:T(8,128)(2,1)}, bf16[128,5120]{1,0:T(8,128)(2,1)}, u32[]{:S(2)}, u32[]{:S(2)}) %collective-permute-start.6) | collective-permute-done | bytes 1310752 | tf_op jit(solution)/shard_map/ppermute | solution.py:18
  295.4 3.8 %fusion.7 = bf16[1,1,128,5120]{3,2,1,0:T(8,128)(2,1)} fusion(f32[128,5120]{1,0:T(8,128)S(1)} %fusion.6, f32[128,5120]{1,0:T(8,128)} %fusion.19, bf16[128,5120]{1,0:T(8,128)(2,1)} %collective-permute-done.6, bf16[4,128,128]{1,2,0:T(8,128)(2,1)S(1)} %collective-permute-done.5), kind=kOutput, calls=%fused_computation.15 | convolution fusion | flops 171048960 | bytes 7897088 | tf_op jit(solution)/shard_map/sn,sd->nd/dot_general | solution.py:147
  299.2 7.9 %reduce-scatter.5.cloned.1.call-done = bf16[2,32,5120]{2,1,0:T(8,128)(2,1)} async-done(((bf16[2,128,5120]{2,1,0:T(8,128)(2,1)}), bf16[2,32,5120]{2,1,0:T(8,128)(2,1)}) %reduce-scatter.5.cloned.1.call-update) | async-done | bytes 655376 | tf_op jit(solution)/shard_map/reduce_scatter | solution.py:248
  307.1 1.2 fusion.88
  308.3 1.9 fusion.92
  310.2 0.9 maximum_bitcast_fusion.1
  311.1 0.9 maximum_bitcast_fusion
  (118 shorter events, 7.5 us)
Async XLA Ops:
  7.2 1.5 copy-start
  7.2 4.3 %copy-start.6 = (bf16[1,1,2,32,5120]{4,3,2,1,0:T(8,128)(2,1)S(1)}, bf16[1,1,2,32,5120]{4,3,2,1,0:T(8,128)(2,1)}, u32[]{:S(2)}) copy-start(bf16[1,1,2,32,5120]{4,3,2,1,0:T(8,128)(2,1)} %param.20) | copy-start | bytes 1966084
  7.2 4.3 %copy-start.21 = (f32[1,1,5120]{2,1,0:T(1,128)S(1)}, f32[1,1,5120]{2,1,0:T(1,128)}, u32[]{:S(2)}) copy-start(f32[1,1,5120]{2,1,0:T(1,128)} %param.15) | copy-start | bytes 61444
  7.2 5.4 %copy-start.17 = (bf16[1,1,32,5120]{3,2,1,0:T(8,128)(2,1)S(1)}, bf16[1,1,32,5120]{3,2,1,0:T(8,128)(2,1)}, u32[]{:S(2)}) copy-start(bf16[1,1,32,5120]{3,2,1,0:T(8,128)(2,1)} %param.19) | copy-start | bytes 983044
  7.2 5.4 %copy-start.12 = (bf16[1,2,32,5120]{3,2,1,0:T(8,128)(2,1)S(1)}, bf16[1,2,32,5120]{3,2,1,0:T(8,128)(2,1)}, u32[]{:S(2)}) copy-start(bf16[1,2,32,5120]{3,2,1,0:T(8,128)(2,1)} %param.21) | copy-start | bytes 1966084
  7.2 85.8 %all-gather.5.cloned.1.call-start = ((), (), s32[]{:S(2)}) async-start(), calls=%async_computation.2 | async-start | bytes 4915200 | tf_op jit(solution)/shard_map/all_gather | solution.py:52
  13.7 141.5 %reduce-scatter.3.cloned.1.call-start = ((), (), s32[]{:S(2)}) async-start(), calls=%async_computation.3 | async-start | bytes 3276800 | tf_op jit(solution)/shard_map/reduce_scatter | solution.py:248
  13.8 6.3 %copy-start.27 = (s32[1,2,5,128]{3,1,2,0:T(2,128)S(1)}, s32[1,2,5,128]{3,1,2,0:T(2,128)}, u32[]{:S(2)}) copy-start(s32[1,2,5,128]{3,1,2,0:T(2,128)} %param.13) | copy-start | bytes 15364
  93.0 4.8 %copy-start.13 = (bf16[1,1,128,5120]{3,2,1,0:T(8,128)(2,1)S(1)}, bf16[1,1,128,5120]{3,2,1,0:T(8,128)(2,1)}, u32[]{:S(2)}) copy-start(bf16[1,1,128,5120]{3,2,1,0:T(8,128)(2,1)} %param.17) | copy-start | bytes 3932164
  93.0 8.3 %copy-start.4 = (bf16[1,384,5120]{2,1,0:T(8,128)(2,1)S(1)}, bf16[1,384,5120]{2,1,0:T(8,128)(2,1)}, u32[]{:S(2)}) copy-start(bf16[1,384,5120]{2,1,0:T(8,128)(2,1)} %pad_bitcast_fusion) | copy-start | bytes 11796484
  97.6 3.6 %copy-start.26 = (bf16[2,3,128,128]{3,2,1,0:T(8,128)(2,1)}, bf16[2,3,128,128]{3,2,1,0:T(8,128)(2,1)S(1)}, u32[]{:S(2)}) copy-start(bf16[2,3,128,128]{3,2,1,0:T(8,128)(2,1)S(1)} %fusion.33) | copy-start | bytes 589828
  97.6 3.7 %copy-start.2 = (bf16[3,128,5120]{2,1,0:T(8,128)(2,1)S(1)}, bf16[3,128,5120]{2,1,0:T(8,128)(2,1)}, u32[]{:S(2)}) copy-start(bf16[3,128,5120]{2,1,0:T(8,128)(2,1)} %copy.15) | copy-start | bytes 11796484
  100.8 3.5 %copy-start.22 = (bf16[1,128,1,128]{1,3,2,0:T(8,128)(2,1)}, bf16[1,128,1,128]{1,3,2,0:T(8,128)(2,1)S(1)}, u32[]{:S(2)}) copy-start(bf16[1,128,1,128]{1,3,2,0:T(8,128)(2,1)S(1)} %fusion.61) | copy-start | bytes 98308
  104.3 85.2 %all-gather.9.cloned.1.call-start = ((), (), s32[]{:S(2)}) async-start(), calls=%async_computation.6 | async-start | bytes 1638400 | tf_op jit(solution)/shard_map/all_gather | solution.py:52
  109.1 60.3 %collective-permute-start = (bf16[2,128,5120]{2,1,0:T(8,128)(2,1)}, bf16[2,128,5120]{2,1,0:T(8,128)(2,1)}, u32[]{:S(2)}, u32[]{:S(2)}) collective-permute-start(bf16[2,128,5120]{2,1,0:T(8,128)(2,1)} %stack.115), channel_id=1, source_target_pairs={{0,25},{1,24},{8,17},{9,16},{16,9},{17,8},{24,1},{25,0},{2,27},{3,... | collective-permute-start | bytes 7864328 | tf_op jit(solution)/shard_map/ppermute | solution.py:18
  156.3 89.7 %all-gather.7.cloned.1.call-start = ((), (), s32[]{:S(2)}) async-start(), calls=%async_computation.4 | async-start | bytes 3276800 | tf_op jit(solution)/shard_map/all_gather | solution.py:52
  156.8 32.9 %copy-start.18 = (bf16[32,5120]{1,0:T(8,128)(2,1)}, bf16[32,5120]{1,0:T(8,128)(2,1)S(1)}, u32[]{:S(2)}) copy-start(bf16[32,5120]{1,0:T(8,128)(2,1)S(1)} %fusion.78) | copy-start | bytes 983044
  156.9 19.3 %collective-permute-start.1 = (bf16[32,5120]{1,0:T(8,128)(2,1)S(1)}, bf16[32,5120]{1,0:T(8,128)(2,1)S(1)}, u32[]{:S(2)}, u32[]{:S(2)}) collective-permute-start(bf16[32,5120]{1,0:T(8,128)(2,1)S(1)} %fusion.78), channel_id=1, source_target_pairs={{1,9},{8,0},{9,17},{16,8},{17,25},{24,16},{3,11},{10,2},{11,19},{1... | collective-permute-start | bytes 983048 | tf_op jit(solution)/shard_map/ppermute | solution.py:262
  159.2 30.3 %copy-start.15 = (bf16[32,5120]{1,0:T(8,128)(2,1)}, bf16[32,5120]{1,0:T(8,128)(2,1)S(1)}, u32[]{:S(2)}) copy-start(bf16[32,5120]{1,0:T(8,128)(2,1)S(1)} %fusion.90) | copy-start | bytes 983044
  159.2 16.9 %collective-permute-start.2 = (bf16[32,5120]{1,0:T(8,128)(2,1)S(1)}, bf16[32,5120]{1,0:T(8,128)(2,1)}, u32[]{:S(2)}, u32[]{:S(2)}) collective-permute-start(bf16[32,5120]{1,0:T(8,128)(2,1)S(1)} %fusion.90), channel_id=1, source_target_pairs={{0,8},{8,16},{9,1},{16,24},{17,9},{25,17},{2,10},{10,18},{11,3},{1... | collective-permute-start | bytes 983048 | tf_op jit(solution)/shard_map/ppermute | solution.py:263
  165.4 10.7 %copy-start.24 = (bf16[128,128]{1,0:T(8,128)(2,1)}, bf16[128,128]{1,0:T(8,128)(2,1)S(1)}, u32[]{:S(2)}) copy-start(bf16[128,128]{1,0:T(8,128)(2,1)S(1)} %convolution_convert_fusion.8) | copy-start | bytes 98308
  176.1 14.7 %copy-start.20 = (bf16[32,5120]{1,0:T(8,128)(2,1)}, bf16[32,5120]{1,0:T(8,128)(2,1)S(1)}, u32[]{:S(2)}) copy-start(bf16[32,5120]{1,0:T(8,128)(2,1)S(1)} %collective-permute-done.1) | copy-start | bytes 983044
  189.5 1.6 copy-start.8
  189.7 7.1 %copy-start.10 = (bf16[32,5120]{1,0:T(8,128)(2,1)}, bf16[32,5120]{1,0:T(8,128)(2,1)S(1)}, u32[]{:S(2)}) copy-start(bf16[32,5120]{1,0:T(8,128)(2,1)S(1)} %get-tuple-element.31) | copy-start | bytes 983044
  190.9 55.1 %copy-start.14 = (bf16[1,1,128,5120]{3,2,1,0:T(8,128)(2,1)S(1)}, bf16[1,1,128,5120]{3,2,1,0:T(8,128)(2,1)}, u32[]{:S(2)}) copy-start(bf16[1,1,128,5120]{3,2,1,0:T(8,128)(2,1)} %param.17) | copy-start | bytes 3932164
  190.9 116.2 %reduce-scatter.5.cloned.1.call-start = ((), (), s32[]{:S(2)}) async-start(), calls=%async_computation.5 | async-start | bytes 3276800 | tf_op jit(solution)/shard_map/reduce_scatter | solution.py:248
  191.1 64.8 %collective-permute-start.3 = (bf16[1,128,5120]{2,1,0:T(8,128)(2,1)S(1)}, bf16[1,128,5120]{2,1,0:T(8,128)(2,1)}, u32[]{:S(2)}, u32[]{:S(2)}) collective-permute-start(bf16[1,128,5120]{2,1,0:T(8,128)(2,1)S(1)} %bitcast.362), channel_id=1, source_target_pairs={{0,25},{1,24},{8,17},{9,16},{16,9},{17,8},{24,1},{25,0},{2,27},{3,... | collective-permute-start | bytes 3932168 | tf_op jit(solution)/shard_map/ppermute | solution.py:18
  192.3 63.6 %collective-permute-start.4 = (bf16[4,128,128]{1,2,0:T(8,128)(2,1)}, bf16[4,128,128]{1,2,0:T(8,128)(2,1)S(1)}, u32[]{:S(2)}, u32[]{:S(2)}) collective-permute-start(bf16[4,128,128]{1,2,0:T(8,128)(2,1)} %pad_maximum_fusion.5), channel_id=1, source_target_pairs={{0,25},{1,24},{8,17},{9,16},{16,9},{17,8},{24,1},{25,0},{2,27},{3,... | collective-permute-start | bytes 393224 | tf_op jit(solution)/shard_map/ppermute | solution.py:18
  246.0 6.9 %copy-start.5 = (bf16[1,384,5120]{2,1,0:T(8,128)(2,1)S(1)}, bf16[1,384,5120]{2,1,0:T(8,128)(2,1)}, u32[]{:S(2)}) copy-start(bf16[1,384,5120]{2,1,0:T(8,128)(2,1)} %pad_bitcast_fusion) | copy-start | bytes 11796484
  248.1 3.5 %copy-start.28 = (s32[128]{0:T(128)S(1)}, s32[128]{0:T(128)}, u32[]{:S(2)}) copy-start(s32[128]{0:T(128)} %get-tuple-element.65) | copy-start | bytes 1540
  248.1 4.7 %copy-start.3 = (bf16[3,128,5120]{2,1,0:T(8,128)(2,1)S(1)}, bf16[3,128,5120]{2,1,0:T(8,128)(2,1)}, u32[]{:S(2)}) copy-start(bf16[3,128,5120]{2,1,0:T(8,128)(2,1)} %copy.15) | copy-start | bytes 11796484
  255.9 0.8 copy-start.25
  256.6 1.8 copy-start.23
  258.5 4.6 %copy-start.11 = (bf16[2,128,5120]{2,1,0:T(8,128)(2,1)S(1)}, bf16[2,128,5120]{2,1,0:T(8,128)(2,1)}, u32[]{:S(2)}) copy-start(bf16[2,128,5120]{2,1,0:T(8,128)(2,1)} %all-gather.7.cloned.1.call-done) | copy-start | bytes 7864324
  261.3 9.0 %collective-permute-start.5 = (bf16[4,128,128]{1,2,0:T(8,128)(2,1)S(1)}, bf16[4,128,128]{1,2,0:T(8,128)(2,1)S(1)}, u32[]{:S(2)}, u32[]{:S(2)}) collective-permute-start(bf16[4,128,128]{1,2,0:T(8,128)(2,1)S(1)} %pad_maximum_fusion.6), channel_id=1, source_target_pairs={{0,25},{1,24},{8,17},{9,16},{16,9},{17,8},{24,1},{25,0},{2,27},{3,... | collective-permute-start | bytes 393224 | tf_op jit(solution)/shard_map/ppermute | solution.py:18
  264.2 1.6 copy-start.9
  264.2 31.3 %collective-permute-start.6 = (bf16[128,5120]{1,0:T(8,128)(2,1)}, bf16[128,5120]{1,0:T(8,128)(2,1)}, u32[]{:S(2)}, u32[]{:S(2)}) collective-permute-start(bf16[128,5120]{1,0:T(8,128)(2,1)} %slice_bitcast_fusion.6), channel_id=1, source_target_pairs={{0,25},{1,24},{8,17},{9,16},{16,9},{17,8},{24,1},{25,0},{2,27},{3,... | collective-permute-start | bytes 3932168 | tf_op jit(solution)/shard_map/ppermute | solution.py:18
  283.5 23.6 %copy-start.7 = (bf16[1,1,2,32,5120]{4,3,2,1,0:T(8,128)(2,1)S(1)}, bf16[1,1,2,32,5120]{4,3,2,1,0:T(8,128)(2,1)}, u32[]{:S(2)}) copy-start(bf16[1,1,2,32,5120]{4,3,2,1,0:T(8,128)(2,1)} %param.20) | copy-start | bytes 1966084
  299.2 11.0 %copy-start.19 = (bf16[32,5120]{1,0:T(8,128)(2,1)S(1)}, bf16[32,5120]{1,0:T(8,128)(2,1)}, u32[]{:S(2)}) copy-start(bf16[32,5120]{1,0:T(8,128)(2,1)} %copy-done.18) | copy-start | bytes 983044
  299.2 11.9 %copy-start.16 = (bf16[32,5120]{1,0:T(8,128)(2,1)S(1)}, bf16[32,5120]{1,0:T(8,128)(2,1)}, u32[]{:S(2)}) copy-start(bf16[32,5120]{1,0:T(8,128)(2,1)} %copy-done.15) | copy-start | bytes 983044
  308.3 3.7 %copy-start.1 = (bf16[64,5120]{1,0:T(8,128)(2,1)S(1)}, bf16[64,5120]{1,0:T(8,128)(2,1)}, u32[]{:S(2)}) copy-start(bf16[64,5120]{1,0:T(8,128)(2,1)} %param.14) | copy-start | bytes 1966084
Sparse Core Ops, SparseCore 0:
  13.8 79.1 all-gather.4
  104.4 50.7 reduce-scatter.2
  157.4 32.0 all-gather.8
  191.5 54.4 all-gather.6
  256.0 51.0 reduce-scatter.4
where the time goes:
time: 320 us; the launch traced here: 319 us
  waiting for transfers between devices  205 us (64%)
  matrix products  47.8 us (15%)
  local copies, waits for them, and re-layouts  24.6 us (8%)
  between operations  14.4 us (4%)
  starting transfers between devices  14.1 us (4%)
  other arithmetic  12.3 us (4%)
    all_gather x3, waiting for transfers between devices, gathered(): full = lax.all_gather(jnp.stack(blocks), 'tp', axis=1, tiled=True)  131 us
    reduce_scatter x2, waiting for transfers between devices, shards(): lax.psum_scatter(both_parts, 'tp', scatter_dimension=1, tiled=True)  52.4 us
    ppermute x5, waiting for transfers between devices, flipped(): lax.ppermute(value, axis, [(i, i ^ mask) for i in range(lax.axis_size(axi...  15.3 us
    dot_general x4, matrix products, weight_terms(): jnp.einsum('sd,csn->cdn', normed_full, d_projected, preferred_element_typ...  10.7 us
    dot_general x4, matrix products, weight_terms(): jnp.einsum('sn,sd->nd', mixed, upstream_full, preferred_element_type=jnp....  9.49 us
    unnamed x59, local copies, waits for them, and re-layouts  7.12 us
    ppermute x5, starting transfers between devices, flipped(): lax.ppermute(value, axis, [(i, i ^ mask) for i in range(lax.axis_size(axi...  7.08 us
    ppermute x1, waiting for transfers between devices, shards(): backward_in = lax.ppermute(backward_out, pair_axes, down_pairs)  6.69 us
  transfers between devices with their start and end apart: 12, of which 8 were waited for; matrix products, arithmetic and copies ran while one was open for 19% of the time, Pallas kernels for 0%

commit v1 on v0

--- a/solution.py
+++ b/solution.py
@@ -49,7 +49,19 @@
 
 
 def gathered(blocks):
-    full = lax.all_gather(jnp.stack(blocks), "tp", axis=1, tiled=True)
+    x = jnp.stack(blocks)
+    ways, here, step = (lax.axis_size("tp"), lax.axis_index("tp"), x.shape[1])
+    shape = [n * ways if d == 1 else n for d, n in enumerate(x.shape)]
+    full = lax.dynamic_update_slice_in_dim(jnp.zeros(shape, x.dtype), x, here * step, axis=1)
+    going_up = going_down = x
+    for far in range(1, ways // 2 + 1):
+        going_up = lax.ppermute(going_up, "tp", [(d, (d + 1) % ways) for d in range(ways)])
+        full = lax.dynamic_update_slice_in_dim(full, going_up, (here - far) % ways * step, axis=1)
+        if 2 * far < ways:
+            going_down = lax.ppermute(going_down, "tp", [(d, (d - 1) % ways) for d in range(ways)])
+            full = lax.dynamic_update_slice_in_dim(
+                full, going_down, (here + far) % ways * step, axis=1
+            )
     return [full[i] for i in range(len(blocks))]
 
 

time: 320 us -> 292 us (0.912)
  waiting for transfers between devices: 205 us -> 147 us
  starting transfers between devices: 14.1 us -> 44 us
  local copies, waits for them, and re-layouts: 24.6 us -> 35.5 us
  matrix products: 47.8 us -> 37.2 us
    all_gather x3 -> x0, waiting for transfers between devices: 131 us -> none  [gathered(): full = lax.all_gather(jnp.stack(blocks), 'tp', axis=1, tiled=True)]
    ppermute x0 -> x9, waiting for transfers between devices: none -> 82.2 us  [the longest x6 67.3 us: gathered(): lax.ppermute(going_up, 'tp', [(d, (d + 1) % ways) for d in range(ways)])]
    ppermute x0 -> x9, starting transfers between devices: none -> 33 us  [the longest x6 25.2 us: gathered(): lax.ppermute(going_up, 'tp', [(d, (d + 1) % ways) for d in range(ways)])]
    dynamic_update_slice x0 -> x10, local copies, waits for them, and re-layouts: none -> 6.78 us  [the longest x6 3.48 us: gathered(): lax.dynamic_update_slice_in_dim(full, going_up, (here - far) % ways * ste...]
    ppermute x1, waiting for transfers between devices: 6.69 us -> 0.01 us  [shards(): backward_in = lax.ppermute(backward_out, pair_axes, down_pairs)]
    ppermute x5, waiting for transfers between devices: 15.3 us -> 10.3 us  [flipped(): lax.ppermute(value, axis, [(i, i ^ mask) for i in range(lax.axis_size(axi...]
    dot_general x2, matrix products: 6.45 us -> 1.72 us  [heads_of(): jnp.einsum('sd,cdn->csn', normed_full, qkv_weight, preferred_element_type...]
    unnamed x59 -> x77, local copies, waits for them, and re-layouts: 7.12 us -> 10.5 us
  transfers between devices with their start and end apart: 12 -> 18, of which waited for: 8 -> 11; matrix products, arithmetic and copies ran while one was open for 19% -> 19% of each run, Pallas kernels for 0% -> 0%
where the time goes in v1:
time: 292 us; the launch traced here: 291 us
  waiting for transfers between devices  147 us (50%)
  starting transfers between devices  44 us (15%)
  matrix products  37.2 us (13%)
  local copies, waits for them, and re-layouts  35.5 us (12%)
  between operations  14.9 us (5%)
  other arithmetic  12.6 us (4%)
    ppermute x6, waiting for transfers between devices, gathered(): lax.ppermute(going_up, 'tp', [(d, (d + 1) % ways) for d in range(ways)])  67.3 us
    reduce_scatter x2, waiting for transfers between devices, shards(): lax.psum_scatter(both_parts, 'tp', scatter_dimension=1, tiled=True)  54.5 us
    ppermute x6, starting transfers between devices, gathered(): lax.ppermute(going_up, 'tp', [(d, (d + 1) % ways) for d in range(ways)])  25.2 us
    ppermute x3, waiting for transfers between devices, gathered(): lax.ppermute(going_down, 'tp', [(d, (d - 1) % ways) for d in range(ways)])  14.9 us
    unnamed x77, local copies, waits for them, and re-layouts  10.5 us
    ppermute x5, waiting for transfers between devices, flipped(): lax.ppermute(value, axis, [(i, i ^ mask) for i in range(lax.axis_size(axi...  10.3 us
    dot_general x4, matrix products, weight_terms(): jnp.einsum('sd,csn->cdn', normed_full, d_projected, preferred_element_typ...  9.37 us
    dot_general x4, matrix products, weight_terms(): jnp.einsum('sn,sd->nd', mixed, upstream_full, preferred_element_type=jnp....  8.84 us
  transfers between devices with their start and end apart: 18, of which 11 were waited for; matrix products, arithmetic and copies ran while one was open for 19% of the time, Pallas kernels for 0%

profile of v1, /device:TPU:0, one launch (start us, length us, event | category | flops | bytes accessed | tf_op | source)
XLA Modules:
  0.0 291.2 jit_solution(2449387656435051768)
XLA Ops:
  8.1 1.3 fusion.71
  9.4 1.5 multiply_reduce_fusion
  13.1 2.3 broadcast_in_dim.35
  15.4 1.5 pad_maximum_fusion.3
  16.9 3.0 %collective-permute-start = (bf16[3,32,5120]{2,1,0:T(8,128)(2,1)}, bf16[3,32,5120]{2,1,0:T(8,128)(2,1)}, u32[]{:S(2)}, u32[]{:S(2)}) collective-permute-start(bf16[3,32,5120]{2,1,0:T(8,128)(2,1)} %get-tuple-element.32), channel_id=1, source_target_pairs={{0,2},{2,4},{4,6},{6,0},{1,3},{3,5},{5,7},{7,1},{8,10},{10,12},{12... | collective-permute-start | bytes 2949128 | tf_op jit(solution)/shard_map/ppermute | solution.py:58
  20.0 2.1 collective-permute-start.1
  22.0 6.5 %copy.15 = bf16[3,128,5120]{2,1,0:T(8,128)(2,1)} copy(bf16[3,128,5120]{1,2,0:T(8,128)(2,1)} %bitcast.363) | data formatting | bytes 7864320 | tf_op jit(solution)/shard_map/transpose | solution.py:130
  29.0 16.0 %collective-permute-done = bf16[3,32,5120]{2,1,0:T(8,128)(2,1)} collective-permute-done((bf16[3,32,5120]{2,1,0:T(8,128)(2,1)}, bf16[3,32,5120]{2,1,0:T(8,128)(2,1)}, u32[]{:S(2)}, u32[]{:S(2)}) %collective-permute-start) | collective-permute-done | bytes 983072 | tf_op jit(solution)/shard_map/ppermute | solution.py:58
  45.0 16.6 %collective-permute-start.2 = (bf16[3,32,5120]{2,1,0:T(8,128)(2,1)}, bf16[3,32,5120]{2,1,0:T(8,128)(2,1)S(1)}, u32[]{:S(2)}, u32[]{:S(2)}) collective-permute-start(bf16[3,32,5120]{2,1,0:T(8,128)(2,1)} %collective-permute-done), channel_id=1, source_target_pairs={{0,2},{2,4},{4,6},{6,0},{1,3},{3,5},{5,7},{7,1},{8,10},{10,12},{12... | collective-permute-start | bytes 2949128 | tf_op jit(solution)/shard_map/ppermute | solution.py:58
  61.6 2.3 constant_dynamic-update-slice_fusion.10
  64.8 2.2 constant_dynamic-update-slice_fusion.9
  67.0 18.2 %collective-permute-done.2 = bf16[3,32,5120]{2,1,0:T(8,128)(2,1)S(1)} collective-permute-done((bf16[3,32,5120]{2,1,0:T(8,128)(2,1)}, bf16[3,32,5120]{2,1,0:T(8,128)(2,1)S(1)}, u32[]{:S(2)}, u32[]{:S(2)}) %collective-permute-start.2) | collective-permute-done | bytes 983072 | tf_op jit(solution)/shard_map/ppermute | solution.py:58
  85.2 1.0 constant_dynamic-update-slice_fusion.8
  86.2 1.8 fusion.67
  88.1 3.4 %fusion.32 = bf16[2,3,128,128]{3,2,1,0:T(8,128)(2,1)S(1)} fusion(bf16[1,1,3,5120,128]{4,3,2,1,0:T(8,128)(2,1)S(1)} %copy-done.6, bf16[3,128,5120]{2,1,0:T(8,128)(2,1)} %constant_dynamic-update-slice_fusion.8), kind=kOutput, calls=%fused_computation.46 | convolution fusion | flops 1006731264 | bytes 6750208 | tf_op jit(solution)/shard_map/tsd,cdn->tcsn/dot_general | solution.py:227
  93.2 3.0 %convolution_convert_fusion.1 = bf16[2,128,5120]{2,1,0:T(8,128)(2,1)} fusion(bf16[1,384,5120]{2,1,0:T(8,128)(2,1)S(1)} %pad_bitcast_fusion, bf16[1,384,5120]{2,1,0:T(8,128)(2,1)S(1)} %bitcast.361, bf16[1,128,384]{1,2,0:T(8,128)(2,1)S(1)} %pad_bitcast_fusion.2, bf16[1,128,384]{1,2,0:T(8,128)(2,1)S(1)} %bitcast.375), kind=kOutput, calls=%fused_computation.5 | convolution fusion | flops 1011974144 | bytes 10682368 | tf_op jit(solution)/shard_map/tsk,tkd->tsd/dot_general | solution.py:146
  98.3 3.5 %stack.115 = bf16[2,128,5120]{2,1,0:T(8,128)(2,1)} slice(bf16[3,128,5120]{2,1,0:T(8,128)(2,1)} %constant_dynamic-update-slice_fusion.8), slice={[0:2], [0:128], [0:5120]} | slice | bytes 5242880 | tf_op jit(solution)/shard_map/stack | solution.py:226
  102.9 46.0 %reduce-scatter.3.cloned.1.call-done = bf16[2,32,5120]{2,1,0:T(8,128)(2,1)} async-done(((bf16[2,128,5120]{2,1,0:T(8,128)(2,1)}), bf16[2,32,5120]{2,1,0:T(8,128)(2,1)}) %reduce-scatter.3.cloned.1.call-update) | async-done | bytes 655376 | tf_op jit(solution)/shard_map/reduce_scatter | solution.py:260
  148.9 1.1 slice_bitcast_fusion.24
  150.5 3.3 %collective-permute-start.4 = (bf16[1,32,5120]{2,1,0:T(8,128)(2,1)}, bf16[1,32,5120]{2,1,0:T(8,128)(2,1)S(1)}, u32[]{:S(2)}, u32[]{:S(2)}) collective-permute-start(bf16[1,32,5120]{2,1,0:T(8,128)(2,1)} %bitcast.50), channel_id=1, source_target_pairs={{0,6},{2,0},{4,2},{6,4},{1,7},{3,1},{5,3},{7,5},{8,14},{10,8},{12,... | collective-permute-start | bytes 983048 | tf_op jit(solution)/shard_map/ppermute | solution.py:61
  155.3 1.3 fusion.77
  156.6 1.3 collective-permute-start.7
  158.0 4.6 %collective-permute-start.8 = (bf16[32,5120]{1,0:T(8,128)(2,1)S(1)}, bf16[32,5120]{1,0:T(8,128)(2,1)S(1)}, u32[]{:S(2)}, u32[]{:S(2)}) collective-permute-start(bf16[32,5120]{1,0:T(8,128)(2,1)S(1)} %fusion.89), channel_id=1, source_target_pairs={{0,8},{8,16},{9,1},{16,24},{17,9},{25,17},{2,10},{10,18},{11,3},{1... | collective-permute-start | bytes 983048 | tf_op jit(solution)/shard_map/ppermute | solution.py:275
  162.7 5.0 %collective-permute-start.5 = (bf16[1,32,5120]{2,1,0:T(8,128)(2,1)S(1)}, bf16[1,32,5120]{2,1,0:T(8,128)(2,1)S(1)}, u32[]{:S(2)}, u32[]{:S(2)}) collective-permute-start(bf16[1,32,5120]{2,1,0:T(8,128)(2,1)S(1)} %collective-permute-done.3), channel_id=1, source_target_pairs={{0,2},{2,4},{4,6},{6,0},{1,3},{3,5},{5,7},{7,1},{8,10},{10,12},{12... | collective-permute-start | bytes 983048 | tf_op jit(solution)/shard_map/ppermute | solution.py:58
  167.8 7.4 %collective-permute-done.5 = bf16[1,32,5120]{2,1,0:T(8,128)(2,1)S(1)} collective-permute-done((bf16[1,32,5120]{2,1,0:T(8,128)(2,1)S(1)}, bf16[1,32,5120]{2,1,0:T(8,128)(2,1)S(1)}, u32[]{:S(2)}, u32[]{:S(2)}) %collective-permute-start.5) | collective-permute-done | bytes 327712 | tf_op jit(solution)/shard_map/ppermute | solution.py:58
  176.3 1.5 copy-done.7
  178.7 2.4 collective-permute-start.10
  181.4 2.6 collective-permute-start.12
  184.0 11.8 %collective-permute-done.9 = bf16[2,32,5120]{2,1,0:T(8,128)(2,1)S(1)} collective-permute-done((bf16[2,32,5120]{2,1,0:T(8,128)(2,1)S(1)}, bf16[2,32,5120]{2,1,0:T(8,128)(2,1)S(1)}, u32[]{:S(2)}, u32[]{:S(2)}) %collective-permute-start.9) | collective-permute-done | bytes 655392 | tf_op jit(solution)/shard_map/ppermute | solution.py:58
  195.8 14.0 %collective-permute-done.10 = bf16[2,32,5120]{2,1,0:T(8,128)(2,1)S(1)} collective-permute-done((bf16[2,32,5120]{2,1,0:T(8,128)(2,1)S(1)}, bf16[2,32,5120]{2,1,0:T(8,128)(2,1)S(1)}, u32[]{:S(2)}, u32[]{:S(2)}) %collective-permute-start.10) | collective-permute-done | bytes 655392 | tf_op jit(solution)/shard_map/ppermute | solution.py:61
  209.9 13.8 %collective-permute-done.11 = bf16[2,32,5120]{2,1,0:T(8,128)(2,1)S(1)} collective-permute-done((bf16[2,32,5120]{2,1,0:T(8,128)(2,1)S(1)}, bf16[2,32,5120]{2,1,0:T(8,128)(2,1)S(1)}, u32[]{:S(2)}, u32[]{:S(2)}) %collective-permute-start.11) | collective-permute-done | bytes 655392 | tf_op jit(solution)/shard_map/ppermute | solution.py:58
  226.8 1.2 copy-done.3
  228.0 3.0 %convolution_convert_fusion = bf16[2,128,5120]{2,1,0:T(8,128)(2,1)} fusion(bf16[1,384,5120]{2,1,0:T(8,128)(2,1)S(1)} %copy-done.5, bf16[1,384,5120]{2,1,0:T(8,128)(2,1)S(1)} %bitcast.362, bf16[1,128,384]{1,2,0:T(8,128)(2,1)S(1)} %pad_bitcast_fusion.1, bf16[1,128,384]{1,2,0:T(8,128)(2,1)S(1)} %bitcast.374), kind=kOutput, calls=%fused_computation.4 | convolution fusion | flops 1011974144 | bytes 10682368 | tf_op jit(solution)/shard_map/tsk,tkd->tsd/dot_general | solution.py:146
  231.3 3.1 %slice_bitcast_fusion.6 = bf16[128,5120]{1,0:T(8,128)(2,1)} fusion(bf16[2,128,5120]{2,1,0:T(8,128)(2,1)} %copy-done.8), kind=kLoop, calls=%fused_computation.32 | loop fusion | bytes 2621440 | tf_op jit(solution)/shard_map/squeeze | solution.py:65
  234.4 2.0 collective-permute-start.15
  236.4 2.0 fusion.110
  238.4 1.2 fusion.23
  239.5 1.9 fusion.18
  241.5 1.2 fusion.20
  242.7 2.6 add_convert_fusion.1
  245.3 4.4 %fusion = bf16[1,1,3,5120,128]{3,4,2,1,0:T(8,128)(2,1)} fusion(bf16[3,128,5120]{2,1,0:T(8,128)(2,1)S(1)} %add_convert_fusion.1, f32[3,128,5120]{2,1,0:T(8,128)S(1)} %fusion.23, bf16[3,128,5120]{2,1,0:T(8,128)(2,1)} %constant_dynamic-update-slice_fusion.8, bf16[1,128,1,128]{1,3,2,0:T(8,128)(2,1)S(1)} %copy-done.34, bf16[1,128,1,128]{1,3,2,0:T(8,128)(2,1)S(1)} %fusion.59, ...), kind=kOutput, calls=%fused_computation.6 | convolution fusion | flops 515211264 | bytes 17137664 | tf_op jit(solution)/shard_map/sd,csn->cdn/dot_general | solution.py:156
  249.7 6.3 %copy.18 = bf16[1,1,3,5120,128]{4,3,2,1,0:T(8,128)(2,1)} copy(bf16[1,1,3,5120,128]{3,4,2,1,0:T(8,128)(2,1)} %fusion) | data formatting | bytes 7864320
  256.0 10.3 %collective-permute-done.15 = bf16[128,5120]{1,0:T(8,128)(2,1)} collective-permute-done((bf16[128,5120]{1,0:T(8,128)(2,1)}, bf16[128,5120]{1,0:T(8,128)(2,1)}, u32[]{:S(2)}, u32[]{:S(2)}) %collective-permute-start.15) | collective-permute-done | bytes 1310752 | tf_op jit(solution)/shard_map/ppermute | solution.py:18
  266.3 1.8 fusion.3
  268.1 3.1 %fusion.7 = bf16[1,1,128,5120]{3,2,1,0:T(8,128)(2,1)} fusion(f32[128,5120]{1,0:T(8,128)S(1)} %fusion.3, f32[128,5120]{1,0:T(8,128)S(1)} %copy-done.10, bf16[3,128,5120]{2,1,0:T(8,128)(2,1)} %constant_dynamic-update-slice_fusion.8, bf16[128,128]{1,0:T(8,128)(2,1)S(1)} %copy-done.36), kind=kOutput, calls=%fused_computation.15 | convolution fusion | flops 171048960 | bytes 7897088 | tf_op jit(solution)/shard_map/sn,sd->nd/dot_general | solution.py:159
  271.3 8.6 %reduce-scatter.5.cloned.1.call-done = bf16[2,32,5120]{2,1,0:T(8,128)(2,1)} async-done(((bf16[2,128,5120]{2,1,0:T(8,128)(2,1)}), bf16[2,32,5120]{2,1,0:T(8,128)(2,1)}) %reduce-scatter.5.cloned.1.call-update) | async-done | bytes 655376 | tf_op jit(solution)/shard_map/reduce_scatter | solution.py:260
  279.8 1.2 fusion.87
  281.1 1.5 fusion.91
  (158 shorter events, 18.6 us)
Async XLA Ops:
  7.2 3.8 %copy-start.11 = (bf16[1,1,2,32,5120]{4,3,2,1,0:T(8,128)(2,1)S(1)}, bf16[1,1,2,32,5120]{4,3,2,1,0:T(8,128)(2,1)}, u32[]{:S(2)}) copy-start(bf16[1,1,2,32,5120]{4,3,2,1,0:T(8,128)(2,1)} %param.20) | copy-start | bytes 1966084
  7.2 3.8 %copy-start.30 = (f32[1,1,5120]{2,1,0:T(1,128)S(1)}, f32[1,1,5120]{2,1,0:T(1,128)}, u32[]{:S(2)}) copy-start(f32[1,1,5120]{2,1,0:T(1,128)} %param.15) | copy-start | bytes 61444
  7.2 3.9 %copy-start.15 = (bf16[1,2,32,5120]{3,2,1,0:T(8,128)(2,1)S(1)}, bf16[1,2,32,5120]{3,2,1,0:T(8,128)(2,1)}, u32[]{:S(2)}) copy-start(bf16[1,2,32,5120]{3,2,1,0:T(8,128)(2,1)} %param.21) | copy-start | bytes 1966084
  7.2 141.7 %reduce-scatter.3.cloned.1.call-start = ((), (), s32[]{:S(2)}) async-start(), calls=%async_computation.2 | async-start | bytes 3276800 | tf_op jit(solution)/shard_map/reduce_scatter | solution.py:260
  16.9 28.1 %collective-permute-start = (bf16[3,32,5120]{2,1,0:T(8,128)(2,1)}, bf16[3,32,5120]{2,1,0:T(8,128)(2,1)}, u32[]{:S(2)}, u32[]{:S(2)}) collective-permute-start(bf16[3,32,5120]{2,1,0:T(8,128)(2,1)} %get-tuple-element.32), channel_id=1, source_target_pairs={{0,2},{2,4},{4,6},{6,0},{1,3},{3,5},{5,7},{7,1},{8,10},{10,12},{12... | collective-permute-start | bytes 2949128 | tf_op jit(solution)/shard_map/ppermute | solution.py:58
  20.0 44.8 %collective-permute-start.1 = (bf16[3,32,5120]{2,1,0:T(8,128)(2,1)}, bf16[3,32,5120]{2,1,0:T(8,128)(2,1)}, u32[]{:S(2)}, u32[]{:S(2)}) collective-permute-start(bf16[3,32,5120]{2,1,0:T(8,128)(2,1)} %get-tuple-element.32), channel_id=1, source_target_pairs={{0,6},{2,0},{4,2},{6,4},{1,7},{3,1},{5,3},{7,5},{8,14},{10,8},{12,... | collective-permute-start | bytes 2949128 | tf_op jit(solution)/shard_map/ppermute | solution.py:61
  22.0 6.5 %copy-start.37 = (s32[1,2,5,128]{3,1,2,0:T(2,128)S(1)}, s32[1,2,5,128]{3,1,2,0:T(2,128)}, u32[]{:S(2)}) copy-start(s32[1,2,5,128]{3,1,2,0:T(2,128)} %param.13) | copy-start | bytes 15364
  22.0 6.5 %copy-start.18 = (bf16[1,1,128,5120]{3,2,1,0:T(8,128)(2,1)S(1)}, bf16[1,1,128,5120]{3,2,1,0:T(8,128)(2,1)}, u32[]{:S(2)}) copy-start(bf16[1,1,128,5120]{3,2,1,0:T(8,128)(2,1)} %param.17) | copy-start | bytes 3932164
  29.0 64.2 %copy-start.4 = (bf16[1,384,5120]{2,1,0:T(8,128)(2,1)}, bf16[1,384,5120]{2,1,0:T(8,128)(2,1)S(1)}, u32[]{:S(2)}) copy-start(bf16[1,384,5120]{2,1,0:T(8,128)(2,1)S(1)} %pad_bitcast_fusion) | copy-start | bytes 11796484
  45.0 40.2 %collective-permute-start.2 = (bf16[3,32,5120]{2,1,0:T(8,128)(2,1)}, bf16[3,32,5120]{2,1,0:T(8,128)(2,1)S(1)}, u32[]{:S(2)}, u32[]{:S(2)}) collective-permute-start(bf16[3,32,5120]{2,1,0:T(8,128)(2,1)} %collective-permute-done), channel_id=1, source_target_pairs={{0,2},{2,4},{4,6},{6,0},{1,3},{3,5},{5,7},{7,1},{8,10},{10,12},{12... | collective-permute-start | bytes 2949128 | tf_op jit(solution)/shard_map/ppermute | solution.py:58
  67.0 21.1 %copy-start.6 = (bf16[1,1,3,5120,128]{4,3,2,1,0:T(8,128)(2,1)S(1)}, bf16[1,1,3,5120,128]{4,3,2,1,0:T(8,128)(2,1)}, u32[]{:S(2)}) copy-start(bf16[1,1,3,5120,128]{4,3,2,1,0:T(8,128)(2,1)} %param.16) | copy-start | bytes 11796484
  88.1 5.1 %copy-start.2 = (bf16[3,128,5120]{2,1,0:T(8,128)(2,1)S(1)}, bf16[3,128,5120]{2,1,0:T(8,128)(2,1)}, u32[]{:S(2)}) copy-start(bf16[3,128,5120]{2,1,0:T(8,128)(2,1)} %copy.15) | copy-start | bytes 11796484
  92.0 4.2 %copy-start.33 = (bf16[1,128,1,128]{1,3,2,0:T(8,128)(2,1)}, bf16[1,128,1,128]{1,3,2,0:T(8,128)(2,1)S(1)}, u32[]{:S(2)}) copy-start(bf16[1,128,1,128]{1,3,2,0:T(8,128)(2,1)S(1)} %fusion.60) | copy-start | bytes 98308
  96.2 183.6 %reduce-scatter.5.cloned.1.call-start = ((), (), s32[]{:S(2)}) async-start(), calls=%async_computation.3 | async-start | bytes 3276800 | tf_op jit(solution)/shard_map/reduce_scatter | solution.py:260
  101.8 53.5 %copy-start.24 = (bf16[1,1,32,5120]{3,2,1,0:T(8,128)(2,1)S(1)}, bf16[1,1,32,5120]{3,2,1,0:T(8,128)(2,1)}, u32[]{:S(2)}) copy-start(bf16[1,1,32,5120]{3,2,1,0:T(8,128)(2,1)} %param.19) | copy-start | bytes 983044
  101.8 73.4 %collective-permute-start.6 = (bf16[2,128,5120]{2,1,0:T(8,128)(2,1)}, bf16[2,128,5120]{2,1,0:T(8,128)(2,1)}, u32[]{:S(2)}, u32[]{:S(2)}) collective-permute-start(bf16[2,128,5120]{2,1,0:T(8,128)(2,1)} %stack.115), channel_id=1, source_target_pairs={{0,25},{1,24},{8,17},{9,16},{16,9},{17,8},{24,1},{25,0},{2,27},{3,... | collective-permute-start | bytes 7864328 | tf_op jit(solution)/shard_map/ppermute | solution.py:18
  102.3 55.7 %copy-start.35 = (bf16[128,128]{1,0:T(8,128)(2,1)}, bf16[128,128]{1,0:T(8,128)(2,1)S(1)}, u32[]{:S(2)}) copy-start(bf16[128,128]{1,0:T(8,128)(2,1)S(1)} %convolution_convert_fusion.8) | copy-start | bytes 98308
  148.9 9.0 %copy-start.31 = (bf16[2,32,5120]{2,1,0:T(8,128)(2,1)S(1)}, bf16[2,32,5120]{2,1,0:T(8,128)(2,1)}, u32[]{:S(2)}) copy-start(bf16[2,32,5120]{2,1,0:T(8,128)(2,1)} %reduce-scatter.3.cloned.1.call-done) | copy-start | bytes 1966084
  150.0 12.7 %collective-permute-start.3 = (bf16[1,32,5120]{2,1,0:T(8,128)(2,1)}, bf16[1,32,5120]{2,1,0:T(8,128)(2,1)S(1)}, u32[]{:S(2)}, u32[]{:S(2)}) collective-permute-start(bf16[1,32,5120]{2,1,0:T(8,128)(2,1)} %bitcast.50), channel_id=1, source_target_pairs={{0,2},{2,4},{4,6},{6,0},{1,3},{3,5},{5,7},{7,1},{8,10},{10,12},{12... | collective-permute-start | bytes 983048 | tf_op jit(solution)/shard_map/ppermute | solution.py:58
  150.5 17.2 %collective-permute-start.4 = (bf16[1,32,5120]{2,1,0:T(8,128)(2,1)}, bf16[1,32,5120]{2,1,0:T(8,128)(2,1)S(1)}, u32[]{:S(2)}, u32[]{:S(2)}) collective-permute-start(bf16[1,32,5120]{2,1,0:T(8,128)(2,1)} %bitcast.50), channel_id=1, source_target_pairs={{0,6},{2,0},{4,2},{6,4},{1,7},{3,1},{5,3},{7,5},{8,14},{10,8},{12,... | collective-permute-start | bytes 983048 | tf_op jit(solution)/shard_map/ppermute | solution.py:61
  155.2 20.1 %copy-start.27 = (bf16[32,5120]{1,0:T(8,128)(2,1)S(1)}, bf16[32,5120]{1,0:T(8,128)(2,1)}, u32[]{:S(2)}) copy-start(bf16[32,5120]{1,0:T(8,128)(2,1)} %fusion.9) | copy-start | bytes 983044
  155.3 20.3 %copy-start.16 = (bf16[1,2,32,5120]{3,2,1,0:T(8,128)(2,1)S(1)}, bf16[1,2,32,5120]{3,2,1,0:T(8,128)(2,1)}, u32[]{:S(2)}) copy-start(bf16[1,2,32,5120]{3,2,1,0:T(8,128)(2,1)} %param.21) | copy-start | bytes 1966084
  156.6 19.0 %copy-start.25 = (bf16[32,5120]{1,0:T(8,128)(2,1)}, bf16[32,5120]{1,0:T(8,128)(2,1)S(1)}, u32[]{:S(2)}) copy-start(bf16[32,5120]{1,0:T(8,128)(2,1)S(1)} %fusion.77) | copy-start | bytes 983044
  156.6 18.7 %collective-permute-start.7 = (bf16[32,5120]{1,0:T(8,128)(2,1)S(1)}, bf16[32,5120]{1,0:T(8,128)(2,1)S(1)}, u32[]{:S(2)}, u32[]{:S(2)}) collective-permute-start(bf16[32,5120]{1,0:T(8,128)(2,1)S(1)} %fusion.77), channel_id=1, source_target_pairs={{1,9},{8,0},{9,17},{16,8},{17,25},{24,16},{3,11},{10,2},{11,19},{1... | collective-permute-start | bytes 983048 | tf_op jit(solution)/shard_map/ppermute | solution.py:274
  158.0 17.3 %copy-start.22 = (bf16[32,5120]{1,0:T(8,128)(2,1)}, bf16[32,5120]{1,0:T(8,128)(2,1)S(1)}, u32[]{:S(2)}) copy-start(bf16[32,5120]{1,0:T(8,128)(2,1)S(1)} %fusion.89) | copy-start | bytes 983044
  158.0 17.3 %collective-permute-start.8 = (bf16[32,5120]{1,0:T(8,128)(2,1)S(1)}, bf16[32,5120]{1,0:T(8,128)(2,1)S(1)}, u32[]{:S(2)}, u32[]{:S(2)}) collective-permute-start(bf16[32,5120]{1,0:T(8,128)(2,1)S(1)} %fusion.89), channel_id=1, source_target_pairs={{0,8},{8,16},{9,1},{16,24},{17,9},{25,17},{2,10},{10,18},{11,3},{1... | collective-permute-start | bytes 983048 | tf_op jit(solution)/shard_map/ppermute | solution.py:275
  162.7 12.5 %collective-permute-start.5 = (bf16[1,32,5120]{2,1,0:T(8,128)(2,1)S(1)}, bf16[1,32,5120]{2,1,0:T(8,128)(2,1)S(1)}, u32[]{:S(2)}, u32[]{:S(2)}) collective-permute-start(bf16[1,32,5120]{2,1,0:T(8,128)(2,1)S(1)} %collective-permute-done.3), channel_id=1, source_target_pairs={{0,2},{2,4},{4,6},{6,0},{1,3},{3,5},{5,7},{7,1},{8,10},{10,12},{12... | collective-permute-start | bytes 983048 | tf_op jit(solution)/shard_map/ppermute | solution.py:58
  176.3 19.5 %collective-permute-start.9 = (bf16[2,32,5120]{2,1,0:T(8,128)(2,1)S(1)}, bf16[2,32,5120]{2,1,0:T(8,128)(2,1)S(1)}, u32[]{:S(2)}, u32[]{:S(2)}) collective-permute-start(bf16[2,32,5120]{2,1,0:T(8,128)(2,1)S(1)} %get-tuple-element.36), channel_id=1, source_target_pairs={{0,2},{2,4},{4,6},{6,0},{1,3},{3,5},{5,7},{7,1},{8,10},{10,12},{12... | collective-permute-start | bytes 1966088 | tf_op jit(solution)/shard_map/ppermute | solution.py:58
  178.7 45.0 %copy-start.19 = (bf16[1,1,128,5120]{3,2,1,0:T(8,128)(2,1)S(1)}, bf16[1,1,128,5120]{3,2,1,0:T(8,128)(2,1)}, u32[]{:S(2)}) copy-start(bf16[1,1,128,5120]{3,2,1,0:T(8,128)(2,1)} %param.17) | copy-start | bytes 3932164
  178.7 31.1 %collective-permute-start.10 = (bf16[2,32,5120]{2,1,0:T(8,128)(2,1)S(1)}, bf16[2,32,5120]{2,1,0:T(8,128)(2,1)S(1)}, u32[]{:S(2)}, u32[]{:S(2)}) collective-permute-start(bf16[2,32,5120]{2,1,0:T(8,128)(2,1)S(1)} %get-tuple-element.36), channel_id=1, source_target_pairs={{0,6},{2,0},{4,2},{6,4},{1,7},{3,1},{5,3},{7,5},{8,14},{10,8},{12,... | collective-permute-start | bytes 1966088 | tf_op jit(solution)/shard_map/ppermute | solution.py:61
  181.3 49.7 %collective-permute-start.13 = (bf16[4,128,128]{1,2,0:T(8,128)(2,1)}, bf16[4,128,128]{1,2,0:T(8,128)(2,1)}, u32[]{:S(2)}, u32[]{:S(2)}) collective-permute-start(bf16[4,128,128]{1,2,0:T(8,128)(2,1)} %pad_maximum_fusion.5), channel_id=1, source_target_pairs={{0,25},{1,24},{8,17},{9,16},{16,9},{17,8},{24,1},{25,0},{2,27},{3,... | collective-permute-start | bytes 393224 | tf_op jit(solution)/shard_map/ppermute | solution.py:18
  181.4 49.6 %collective-permute-start.12 = (bf16[1,128,5120]{2,1,0:T(8,128)(2,1)S(1)}, bf16[1,128,5120]{2,1,0:T(8,128)(2,1)S(1)}, u32[]{:S(2)}, u32[]{:S(2)}) collective-permute-start(bf16[1,128,5120]{2,1,0:T(8,128)(2,1)S(1)} %constant_dynamic-update-slice_fusion.4), channel_id=1, source_target_pairs={{0,25},{1,24},{8,17},{9,16},{16,9},{17,8},{24,1},{25,0},{2,27},{3,... | collective-permute-start | bytes 3932168 | tf_op jit(solution)/shard_map/ppermute | solution.py:18
  195.8 27.9 %collective-permute-start.11 = (bf16[2,32,5120]{2,1,0:T(8,128)(2,1)S(1)}, bf16[2,32,5120]{2,1,0:T(8,128)(2,1)S(1)}, u32[]{:S(2)}, u32[]{:S(2)}) collective-permute-start(bf16[2,32,5120]{2,1,0:T(8,128)(2,1)S(1)} %collective-permute-done.9), channel_id=1, source_target_pairs={{0,2},{2,4},{4,6},{6,0},{1,3},{3,5},{5,7},{7,1},{8,10},{10,12},{12... | collective-permute-start | bytes 1966088 | tf_op jit(solution)/shard_map/ppermute | solution.py:58
  223.7 3.1 %copy-start.5 = (bf16[1,384,5120]{2,1,0:T(8,128)(2,1)S(1)}, bf16[1,384,5120]{2,1,0:T(8,128)(2,1)}, u32[]{:S(2)}) copy-start(bf16[1,384,5120]{2,1,0:T(8,128)(2,1)} %copy-done.4) | copy-start | bytes 11796484
  224.2 3.7 %copy-start.3 = (bf16[3,128,5120]{2,1,0:T(8,128)(2,1)S(1)}, bf16[3,128,5120]{2,1,0:T(8,128)(2,1)}, u32[]{:S(2)}) copy-start(bf16[3,128,5120]{2,1,0:T(8,128)(2,1)} %copy.15) | copy-start | bytes 11796484
  230.9 3.4 %copy-start.20 = (bf16[1,128,5120]{2,1,0:T(8,128)(2,1)}, bf16[1,128,5120]{2,1,0:T(8,128)(2,1)S(1)}, u32[]{:S(2)}) copy-start(bf16[1,128,5120]{2,1,0:T(8,128)(2,1)S(1)} %collective-permute-done.12) | copy-start | bytes 3932164
  231.0 5.4 %copy-start.9 = (bf16[2,128,5120]{2,1,0:T(8,128)(2,1)S(1)}, bf16[2,128,5120]{2,1,0:T(8,128)(2,1)}, u32[]{:S(2)}) copy-start(bf16[2,128,5120]{2,1,0:T(8,128)(2,1)} %copy-done.8) | copy-start | bytes 7864324
  231.2 10.3 %collective-permute-start.14 = (bf16[4,128,128]{1,2,0:T(8,128)(2,1)S(1)}, bf16[4,128,128]{1,2,0:T(8,128)(2,1)S(1)}, u32[]{:S(2)}, u32[]{:S(2)}) collective-permute-start(bf16[4,128,128]{1,2,0:T(8,128)(2,1)S(1)} %pad_maximum_fusion.6), channel_id=1, source_target_pairs={{0,25},{1,24},{8,17},{9,16},{16,9},{17,8},{24,1},{25,0},{2,27},{3,... | collective-permute-start | bytes 393224 | tf_op jit(solution)/shard_map/ppermute | solution.py:18
  234.4 31.9 %collective-permute-start.15 = (bf16[128,5120]{1,0:T(8,128)(2,1)}, bf16[128,5120]{1,0:T(8,128)(2,1)}, u32[]{:S(2)}, u32[]{:S(2)}) collective-permute-start(bf16[128,5120]{1,0:T(8,128)(2,1)} %slice_bitcast_fusion.6), channel_id=1, source_target_pairs={{0,25},{1,24},{8,17},{9,16},{16,9},{17,8},{24,1},{25,0},{2,27},{3,... | collective-permute-start | bytes 3932168 | tf_op jit(solution)/shard_map/ppermute | solution.py:18
  256.0 12.1 %copy-start.10 = (f32[128,5120]{1,0:T(8,128)S(1)}, f32[128,5120]{1,0:T(8,128)}, u32[]{:S(2)}) copy-start(f32[128,5120]{1,0:T(8,128)} %fusion.110) | copy-start | bytes 7864324
  256.0 12.1 %copy-start.36 = (bf16[128,128]{1,0:T(8,128)(2,1)S(1)}, bf16[128,128]{1,0:T(8,128)(2,1)}, u32[]{:S(2)}) copy-start(bf16[128,128]{1,0:T(8,128)(2,1)} %copy-done.35) | copy-start | bytes 98308
  268.1 11.7 %copy-start.12 = (bf16[1,1,2,32,5120]{4,3,2,1,0:T(8,128)(2,1)S(1)}, bf16[1,1,2,32,5120]{4,3,2,1,0:T(8,128)(2,1)}, u32[]{:S(2)}) copy-start(bf16[1,1,2,32,5120]{4,3,2,1,0:T(8,128)(2,1)} %param.20) | copy-start | bytes 1966084
  268.1 12.9 %copy-start.14 = (bf16[32,5120]{1,0:T(8,128)(2,1)S(1)}, bf16[32,5120]{1,0:T(8,128)(2,1)}, u32[]{:S(2)}) copy-start(bf16[32,5120]{1,0:T(8,128)(2,1)} %copy-done.13) | copy-start | bytes 983044
  268.1 12.9 %copy-start.17 = (bf16[1,2,32,5120]{3,2,1,0:T(8,128)(2,1)S(1)}, bf16[1,2,32,5120]{3,2,1,0:T(8,128)(2,1)}, u32[]{:S(2)}) copy-start(bf16[1,2,32,5120]{3,2,1,0:T(8,128)(2,1)} %param.21) | copy-start | bytes 1966084
  268.1 12.9 %copy-start.29 = (bf16[32,5120]{1,0:T(8,128)(2,1)S(1)}, bf16[32,5120]{1,0:T(8,128)(2,1)}, u32[]{:S(2)}) copy-start(bf16[32,5120]{1,0:T(8,128)(2,1)} %copy-done.28) | copy-start | bytes 983044
  271.3 11.3 %copy-start.26 = (bf16[32,5120]{1,0:T(8,128)(2,1)S(1)}, bf16[32,5120]{1,0:T(8,128)(2,1)}, u32[]{:S(2)}) copy-start(bf16[32,5120]{1,0:T(8,128)(2,1)} %copy-done.25) | copy-start | bytes 983044
  271.3 12.2 %copy-start.23 = (bf16[32,5120]{1,0:T(8,128)(2,1)S(1)}, bf16[32,5120]{1,0:T(8,128)(2,1)}, u32[]{:S(2)}) copy-start(bf16[32,5120]{1,0:T(8,128)(2,1)} %copy-done.22) | copy-start | bytes 983044
  281.0 3.3 %copy-start.1 = (bf16[64,5120]{1,0:T(8,128)(2,1)S(1)}, bf16[64,5120]{1,0:T(8,128)(2,1)}, u32[]{:S(2)}) copy-start(bf16[64,5120]{1,0:T(8,128)(2,1)} %param.14) | copy-start | bytes 1966084
  (8 other events, 13.1 us)
Sparse Core Ops, SparseCore 0:
  96.3 52.5 reduce-scatter.2
  231.1 48.6 reduce-scatter.4
